TPU v7x, 32 devices: a whole 2x2x4 slice. The times are simulated.
32 devices in a mesh: leaf: 8 (over z, y), panel: 4 (over x, core).
Axes of the slice: x: 2, y: 2, z: 4, core: 2. Of those that a mesh axis runs over, the one named last changes fastest.
Arguments:
- interface_block: float32 [8, 2048, 2048], P('leaf', 'panel'), may hold values from -0.125 to 0.125
- coupling: bfloat16 [8, 2048, 128], P('leaf', 'panel'), may hold values from -0.375 to 0.375
- eigenvalues: float32 [8, 128], P('leaf'), may hold values from 0.5 to 8
- mode_counts: int32 [8], P('leaf'), may hold values from 64 to 128, as said below
- interface_coords: bfloat16 [8, 2048, 1024], P('leaf', 'panel'), may hold values from -6 to 6
- modal_coords: bfloat16 [8, 128, 4096], P('leaf'), may hold values from -6 to 6
Outputs:
- mode_shapes: float32 [8, 2048, 1024], P('leaf', 'panel')
Inputs may be any that keep to these rules, and one draw needn't show every extreme that they name: `mode_counts`: modes kept by each substructure; some substructure keeps all 128.
All inputs are finite; a program needn't handle non-finite values.
Results may differ from a plain program's by a relative error of at most 0.0023.
Values may be sent and summed in bfloat16 or wider, within the bound.
No kernel may reach another device: no remote copies, remote signals or barrier semaphores. Data moves between devices by JAX's collectives and lax.ppermute only.
A program may use at most 128 MiB of HBM per device.

v0:
```python
import jax
import jax.numpy as jnp
from jax import lax
from jax.sharding import PartitionSpec as P

LEVELS = 2


def partner(value, axis, bit):
    return lax.ppermute(value, axis, [(i, i ^ 1 << bit) for i in range(lax.axis_size(axis))])


def modal_reduce(summed, levels):
    leaf_index = lax.axis_index("leaf")
    current = summed
    for level in range(levels - 1, -1, -1):
        half = current.shape[1] // 2
        my_bit = leaf_index >> level & 1
        keep = lax.dynamic_slice_in_dim(current, my_bit * half, half, 1)
        other = lax.dynamic_slice_in_dim(current, (1 - my_bit) * half, half, 1)
        current = keep + partner(other, "leaf", level)
    return current


def on_device(interface_block, coupling, eigenvalues, mode_counts, interface_coords, modal_coords):
    block = interface_block[0]
    coup = coupling[0]
    coords = interface_coords[0]
    modal = modal_coords[0]
    width = coup.shape[1]
    levels = LEVELS
    index = jnp.arange(width, dtype=jnp.int32)
    mask = (index < mode_counts[0]).astype(jnp.float32)
    scaled = (coup.astype(jnp.float32) * (mask / eigenvalues[0])[None, :]).astype(jnp.bfloat16)
    columns = block
    schur = columns - lax.dot_general(
        scaled,
        lax.all_gather(coup, "panel", axis=0, tiled=True),
        (((1,), (1,)), ((), ())),
        preferred_element_type=jnp.float32,
    )
    merged = schur
    for level in range(levels):
        merged = merged + partner(merged, "leaf", level)
    owned = modal_reduce(jnp.dot(scaled, modal, preferred_element_type=jnp.float32), levels)
    columns = merged
    shapes = owned + jnp.dot(
        columns,
        lax.all_gather(coords, "panel", axis=0, tiled=True).astype(jnp.float32),
        precision=lax.Precision.HIGHEST,
    )
    return shapes[None]


def solution(mesh):
    placed = (
        P("leaf", "panel", None),
        P("leaf", "panel", None),
        P("leaf", None),
        P("leaf"),
        P("leaf", "panel", None),
        P("leaf", None, None),
    )
    return jax.shard_map(
        on_device, mesh=mesh, in_specs=placed, out_specs=P("leaf", "panel", None), check_vma=False
    )
```

profile of v0, /device:TPU:0, one launch (start us, length us, event | category | flops | bytes accessed | tf_op | source)
XLA Modules:
  0.0 233.8 jit_solution(16396193473058666457)
XLA Ops:
  6.5 0.0 copy-start
  6.5 0.0 all-gather.4.cloned.1.call-start
  7.3 8.9 %all-gather = bf16[1,2048,128]{2,1,0:T(8,128)(2,1)S(1)} all-gather(bf16[1,512,128]{2,1,0:T(8,128)(2,1)} %param.7), channel_id=2, replica_groups=mesh['leaf'=8,'panel'=4] {'panel'}, dimensions={1}, use_global_device_ids=true | all-gather | bytes 655360 | tf_op jit(solution)/shard_map/all_gather | solution.py:38
  16.1 0.7 fusion.15
  16.8 5.0 %bitcast_subtract_fusion = f32[512,2048]{1,0:T(8,128)} fusion(f32[1,512,2048]{2,1,0:T(8,128)} %param.6, bf16[1,2048,128]{2,1,0:T(8,128)(2,1)S(1)} %all-gather, bf16[1,512,128]{2,1,0:T(8,128)(2,1)} %param.7, f32[128]{0:T(128)S(1)} %fusion.15), kind=kOutput, calls=%fused_computation.2 | convolution fusion | flops 269680640 | bytes 9044480 | tf_op jit(solution)/shard_map/dot_general | solution.py:36
  21.8 1.5 collective-permute-start.2
  23.3 0.0 copy-done
  23.3 0.0 copy-done.3
  23.3 1.2 fusion.3
  24.6 2.4 %constant_dynamic-slice_fusion.1 = f32[512,2048]{1,0:T(8,128)} fusion(f32[512,4096]{1,0:T(8,128)S(1)} %fusion.3, s32[]{:T(128)S(6)} %select_n.13), kind=kLoop, calls=%fused_computation.19 | loop fusion | bytes 8388612 | tf_op jit(solution)/shard_map/dynamic_slice | solution.py:20
  27.0 2.1 copy-done.1
  29.1 1.6 collective-permute-start
  30.7 0.0 all-gather.4.cloned.1.call-update
  30.7 84.2 %collective-permute-done.2 = f32[512,2048]{1,0:T(8,128)} collective-permute-done((f32[512,2048]{1,0:T(8,128)}, f32[512,2048]{1,0:T(8,128)}, u32[]{:S(2)}, u32[]{:S(2)}) %collective-permute-start.2) | collective-permute-done | bytes 4194336 | tf_op jit(solution)/shard_map/ppermute | solution.py:10
  114.9 6.5 %add.33 = f32[512,2048]{1,0:T(8,128)} add(f32[512,2048]{1,0:T(8,128)} %bitcast_subtract_fusion, f32[512,2048]{1,0:T(8,128)} %collective-permute-done.2) | non-fusion elementwise | flops 1048576 | bytes 12582912 | tf_op jit(solution)/shard_map/add | solution.py:44
  121.4 1.6 collective-permute-start.3
  123.0 0.0 collective-permute-done
  123.0 4.2 %dynamic-slice_add_fusion = f32[512,2048]{1,0:T(8,128)S(1)} fusion(f32[512,2048]{1,0:T(8,128)} %collective-permute-done, f32[512,4096]{1,0:T(8,128)} %copy-done.1, s32[]{:T(128)S(6)} %select_n.12), kind=kLoop, calls=%fused_computation.4 | loop fusion | flops 1048576 | bytes 12582916 | tf_op jit(solution)/shard_map/add | solution.py:21
  127.3 1.9 copy-done.2
  129.2 0.1 constant_dynamic-slice_fusion
  129.3 1.6 collective-permute-start.1
  130.9 45.3 %collective-permute-done.1 = f32[512,1024]{1,0:T(8,128)} collective-permute-done((f32[512,1024]{1,0:T(8,128)S(1)}, f32[512,1024]{1,0:T(8,128)}, u32[]{:S(2)}, u32[]{:S(2)}) %collective-permute-start.1) | collective-permute-done | bytes 2097184 | tf_op jit(solution)/shard_map/ppermute | solution.py:10
  176.2 37.5 %collective-permute-done.3 = f32[512,2048]{1,0:T(8,128)} collective-permute-done((f32[512,2048]{1,0:T(8,128)}, f32[512,2048]{1,0:T(8,128)}, u32[]{:S(2)}, u32[]{:S(2)}) %collective-permute-start.3) | collective-permute-done | bytes 4194336 | tf_op jit(solution)/shard_map/ppermute | solution.py:10
  213.7 13.3 %add_bitcast_fusion = f32[1,512,1024]{2,1,0:T(8,128)} fusion(f32[512,1024]{1,0:T(8,128)} %collective-permute-done.1, f32[512,2048]{1,0:T(8,128)} %copy-done.2, s32[]{:T(128)S(6)} %select_n.14, bf16[1,2048,1024]{2,1,0:T(8,128)(2,1)} %all-gather.4.cloned.1.call-done, f32[512,2048]{1,0:T(8,128)} %add.33, f32[512,2048]{1,0:T(8,128)} %collective-permute-done.3), kind=kOutput, calls=%fused_computation.5 | convolution fusion | flops 12886999040 | bytes 18874372 | tf_op jit(solution)/shard_map/dot_general | solution.py:47
  (4 shorter events, 0.0 us)
Async XLA Ops:
  6.5 16.8 %copy-start = (bf16[1,128,4096]{2,1,0:T(8,128)(2,1)S(1)}, bf16[1,128,4096]{2,1,0:T(8,128)(2,1)}, u32[]{:S(2)}) copy-start(bf16[1,128,4096]{2,1,0:T(8,128)(2,1)} %param.11) | copy-start | bytes 3145732
  6.5 169.7 %all-gather.4.cloned.1.call-start = ((), (), s32[]{:S(2)}) async-start(), calls=%async_computation | async-start | bytes 5242880 | tf_op jit(solution)/shard_map/all_gather | solution.py:49
  16.8 6.5 %copy-start.3 = (bf16[1,512,128]{2,1,0:T(8,128)(2,1)S(1)}, bf16[1,512,128]{2,1,0:T(8,128)(2,1)}, u32[]{:S(2)}) copy-start(bf16[1,512,128]{2,1,0:T(8,128)(2,1)} %param.7) | copy-start | bytes 393220
  21.8 93.1 %collective-permute-start.2 = (f32[512,2048]{1,0:T(8,128)}, f32[512,2048]{1,0:T(8,128)}, u32[]{:S(2)}, u32[]{:S(2)}) collective-permute-start(f32[512,2048]{1,0:T(8,128)} %bitcast_subtract_fusion), channel_id=1, source_target_pairs={{0,4},{4,0},{8,12},{12,8},{16,20},{20,16},{24,28},{28,24},{1,5},{5... | collective-permute-start | bytes 12582920 | tf_op jit(solution)/shard_map/ppermute | solution.py:10
  24.6 4.5 %copy-start.1 = (f32[512,4096]{1,0:T(8,128)}, f32[512,4096]{1,0:T(8,128)S(1)}, u32[]{:S(2)}) copy-start(f32[512,4096]{1,0:T(8,128)S(1)} %fusion.3) | copy-start | bytes 25165828
  29.1 93.9 %collective-permute-start = (f32[512,2048]{1,0:T(8,128)}, f32[512,2048]{1,0:T(8,128)}, u32[]{:S(2)}, u32[]{:S(2)}) collective-permute-start(f32[512,2048]{1,0:T(8,128)} %constant_dynamic-slice_fusion.1), channel_id=1, source_target_pairs={{0,8},{4,12},{8,0},{12,4},{16,24},{20,28},{24,16},{28,20},{1,9},{5... | collective-permute-start | bytes 12582920 | tf_op jit(solution)/shard_map/ppermute | solution.py:10
  121.4 92.3 %collective-permute-start.3 = (f32[512,2048]{1,0:T(8,128)}, f32[512,2048]{1,0:T(8,128)}, u32[]{:S(2)}, u32[]{:S(2)}) collective-permute-start(f32[512,2048]{1,0:T(8,128)} %add.33), channel_id=1, source_target_pairs={{0,8},{4,12},{8,0},{12,4},{16,24},{20,28},{24,16},{28,20},{1,9},{5... | collective-permute-start | bytes 12582920 | tf_op jit(solution)/shard_map/ppermute | solution.py:10
  127.3 1.9 copy-start.2
  129.3 46.9 %collective-permute-start.1 = (f32[512,1024]{1,0:T(8,128)S(1)}, f32[512,1024]{1,0:T(8,128)}, u32[]{:S(2)}, u32[]{:S(2)}) collective-permute-start(f32[512,1024]{1,0:T(8,128)S(1)} %constant_dynamic-slice_fusion), channel_id=1, source_target_pairs={{0,4},{4,0},{8,12},{12,8},{16,20},{20,16},{24,28},{28,24},{1,5},{5... | collective-permute-start | bytes 6291464 | tf_op jit(solution)/shard_map/ppermute | solution.py:10
Sparse Core Ops, SparseCore 0:
  30.8 33.3 all-gather.3
where the time goes:
time: 234 us
  waiting for transfers between devices  167 us (71%)
  matrix products  19.5 us (8%)
  between operations  14.2 us (6%)
  other arithmetic  11.4 us (5%)
  blocking collectives  8.86 us (4%)
  local copies, waits for them, and re-layouts  6.59 us (3%)
  starting transfers between devices  6.26 us (3%)
    ppermute x4, waiting for transfers between devices, partner(): lax.ppermute(value, axis, [(i, i ^ 1 << bit) for i in range(lax.axis_size...  167 us
    dot_general x1, matrix products, on_device(): jnp.dot(columns, lax.all_gather(coords, 'panel', axis=0, tiled=True).asty...  13.3 us
    all_gather x1, blocking collectives, on_device(): lax.all_gather(coup, 'panel', axis=0, tiled=True)  8.86 us
    add x1, other arithmetic, on_device(): merged = merged + partner(merged, 'leaf', level)  6.52 us
    ppermute x4, starting transfers between devices, partner(): lax.ppermute(value, axis, [(i, i ^ 1 << bit) for i in range(lax.axis_size...  6.26 us
    dot_general x1, matrix products, on_device(): lax.dot_general(scaled, lax.all_gather(coup, 'panel', axis=0, tiled=True)...  4.98 us
  transfers between devices with their start and end apart: 5, of which 3 were waited for; matrix products, arithmetic and copies ran while one was open for 6% of the time, Pallas kernels for 0%

commit v1 on v0

v1 whole, which is shorter than its diff:
```python
import jax
import jax.numpy as jnp
from jax import lax
from jax.sharding import Mesh, PartitionSpec as P


def on_device(interface_block, coupling, eigenvalues, mode_counts, interface_coords, modal_coords):
    block = interface_block[0]
    coup = coupling[0]
    coords = interface_coords[0]
    modal = modal_coords[0]
    width = coup.shape[1]
    group = lax.axis_size("leafin")
    index = jnp.arange(width, dtype=jnp.int32)
    mask = (index < mode_counts[0]).astype(jnp.float32)
    scaled = (coup.astype(jnp.float32) * (mask / eigenvalues[0])[None, :]).astype(jnp.bfloat16)
    dense = lax.psum(block, "leafin")
    scaled_all = lax.all_gather(scaled, "leafin", axis=1, tiled=True)
    coup_rows = lax.all_gather(coup, "panel", axis=0, tiled=True)
    coup_all = lax.all_gather(coup_rows, "leafin", axis=1, tiled=True)
    low = lax.dot_general(scaled_all, coup_all, (((1,), (1,)), ((), ())), preferred_element_type=jnp.float32)
    merged = dense - low
    rl = modal.shape[1] // group
    parts = jnp.transpose(modal.reshape(modal.shape[0], group, rl), (1, 0, 2))
    recv = lax.all_to_all(parts, "leafin", 0, 0, tiled=True)
    modal_term = jnp.dot(scaled_all, recv.reshape(group * modal.shape[0], rl), preferred_element_type=jnp.float32)
    coords_all = lax.all_gather(coords, "panel", axis=0, tiled=True)
    shapes = modal_term + jnp.dot(merged, coords_all.astype(jnp.float32), precision=lax.Precision.HIGHEST)
    return shapes[None]


def solution(mesh):
    def run(*args):
        group = args[5].shape[2] // args[4].shape[2]
        leaves, panels = mesh.shape["leaf"], mesh.shape["panel"]
        grid = mesh.devices.reshape(leaves // group, group, panels)
        sub = Mesh(grid, ("grp", "leafin", "panel"))
        leaf = ("grp", "leafin")
        placed = (
            P(leaf, "panel", None),
            P(leaf, "panel", None),
            P(leaf, None),
            P(leaf),
            P(leaf, "panel", None),
            P(leaf, None, None),
        )
        body = jax.shard_map(on_device, mesh=sub, in_specs=placed, out_specs=P(leaf, "panel", None), check_vma=False)
        return body(*args)

    return run
```

time: 234 us -> 296 us (1.26)
  blocking collectives: 8.86 us -> 68.2 us
  waiting for transfers between devices: 167 us -> 190 us
  other arithmetic: 11.4 us -> 0.04 us
  local copies, waits for them, and re-layouts: 6.59 us -> 1.85 us
    ppermute x4 -> x0, waiting for transfers between devices: 167 us -> none  [partner(): lax.ppermute(value, axis, [(i, i ^ 1 << bit) for i in range(lax.axis_size...]
    psum x0 -> x1, waiting for transfers between devices: none -> 153 us  [on_device(): dense = lax.psum(block, 'leafin')]
    all_gather x1 -> x2, blocking collectives: 8.86 us -> 68.2 us  [the longest x1 57.9 us: on_device(): scaled_all = lax.all_gather(scaled, 'leafin', axis=1, tiled=True)]
    all_gather x1 -> x2, waiting for transfers between devices: 0.01 us -> 35.9 us  [the longest x1 35.9 us: on_device(): coords_all = lax.all_gather(coords, 'panel', axis=0, tiled=True)]
    add x2 -> x0, other arithmetic: 10.7 us -> none  [the longest x1 6.52 us: on_device(): merged = merged + partner(merged, 'leaf', level)]
    ppermute x4 -> x0, starting transfers between devices: 6.26 us -> none  [partner(): lax.ppermute(value, axis, [(i, i ^ 1 << bit) for i in range(lax.axis_size...]
    all_to_all x0 -> x1, starting transfers between devices: none -> 3.8 us  [on_device(): recv = lax.all_to_all(parts, 'leafin', 0, 0, tiled=True)]
  transfers between devices with their start and end apart: 5 -> 4, of which waited for: 3 -> 2; matrix products, arithmetic and copies ran while one was open for 6% -> 2% of each run, Pallas kernels for 0% -> 0%
where the time goes in v1:
time: 296 us; the launch traced here: 295 us
  waiting for transfers between devices  190 us (64%)
  blocking collectives  68.2 us (23%)
  matrix products  17.3 us (6%)
  between operations  13.8 us (5%)
  starting transfers between devices  3.88 us (1%)
    psum x1, waiting for transfers between devices, on_device(): dense = lax.psum(block, 'leafin')  153 us
    all_gather x1, blocking collectives, on_device(): scaled_all = lax.all_gather(scaled, 'leafin', axis=1, tiled=True)  57.9 us
    all_gather x1, waiting for transfers between devices, on_device(): coords_all = lax.all_gather(coords, 'panel', axis=0, tiled=True)  35.9 us
    dot_general x1, matrix products, on_device(): jnp.dot(merged, coords_all.astype(jnp.float32), precision=lax.Precision.H...  10.5 us
    all_gather x1, blocking collectives, on_device(): coup_rows = lax.all_gather(coup, 'panel', axis=0, tiled=True)  10.3 us
  transfers between devices with their start and end apart: 4, of which 2 were waited for; matrix products, arithmetic and copies ran while one was open for 2% of the time, Pallas kernels for 0%

profile of v1, /device:TPU:0, one launch (start us, length us, event | category | flops | bytes accessed | tf_op | source)
XLA Modules:
  0.0 295.3 jit_solution(14571388144809049129)
XLA Ops:
  6.5 0.0 copy-start
  6.5 0.0 all-gather.6.cloned.1.call-start
  6.5 10.3 %all-gather = bf16[1,2048,128]{2,1,0:T(8,128)(2,1)} all-gather(bf16[1,512,128]{2,1,0:T(8,128)(2,1)} %param.7), channel_id=2, replica_groups=mesh['grp'=2,'leafin'=4,'panel'=4] {'panel'}, dimensions={1}, use_global_device_ids=true | all-gather | bytes 655360 | tf_op jit(solution)/shard_map/all_gather | solution.py:19
  16.9 0.0 all-gather.6.cloned.1.call-update
  16.9 0.0 all-reduce.2.cloned.1.call-start
  16.9 0.0 copy-start.2
  16.9 0.0 copy-start.1
  17.0 0.7 all-reduce.2.cloned.1.call-update
  17.6 0.0 all-gather.8.cloned.1.call-start
  17.7 0.7 all-gather.8.cloned.1.call-update
  18.4 0.0 copy-done
  18.4 1.3 copy.7
  19.7 3.8 %all-to-all-start = ((bf16[4,128,1024]{1,2,0:T(8,128)(2,1)}), bf16[4,128,1024]{1,2,0:T(8,128)(2,1)S(1)}, u32[]{:S(2)}, u32[]{:S(2)}) async-start(bf16[4,128,1024]{1,2,0:T(8,128)(2,1)} %bitcast.4), calls=%async_computation | async-start | bytes 2097152 | tf_op jit(solution)/shard_map/all_to_all | solution.py:25
  24.1 0.0 copy-done.2
  24.2 0.0 copy-done.1
  24.2 57.9 %all_gather.12 = bf16[512,512]{1,0:T(8,128)(2,1)S(1)} all-gather(bf16[512,128]{1,0:T(8,128)(2,1)S(1)} %fusion.5), channel_id=1, replica_groups=mesh['grp'=2,'leafin'=4,'panel'=4] {'leafin'}, dimensions={1}, use_global_device_ids=true | all-gather | bytes 655360 | tf_op jit(solution)/shard_map/all_gather | solution.py:18
  82.1 0.0 all-to-all-done
  82.1 0.5 copy.8
  82.6 0.0 all-gather.6.cloned.1.call-done
  82.7 4.8 %fusion.3 = f32[512,2048]{1,0:T(8,128)} fusion(bf16[512,512]{1,0:T(8,128)(2,1)S(1)} %all_gather.12, bf16[1,2048,512]{2,1,0:T(8,128)(2,1)} %all-gather.6.cloned.1.call-done), kind=kOutput, calls=%fused_computation.3 | convolution fusion | flops 1073741824 | bytes 6815744 | tf_op jit(solution)/shard_map/dot_general | solution.py:21
  87.5 152.8 %all-reduce.2.cloned.1.call-done = f32[512,2048]{1,0:T(8,128)} async-done(((f32[512,2048]{1,0:T(8,128)}), f32[512,2048]{1,0:T(8,128)}) %all-reduce.2.cloned.1.call-update) | async-done | bytes 4194320 | tf_op jit(solution)/shard_map/psum | solution.py:17
  240.3 35.9 %all-gather.8.cloned.1.call-done = bf16[1,2048,1024]{2,1,0:T(8,128)(2,1)} async-done(((bf16[1,512,1024]{2,1,0:T(8,128)(2,1)}), bf16[1,2048,1024]{2,1,0:T(8,128)(2,1)}) %all-gather.8.cloned.1.call-update) | async-done | bytes 4194320 | tf_op jit(solution)/shard_map/all_gather | solution.py:27
  276.3 10.5 %fusion = f32[512,1024]{1,0:T(8,128)S(1)} fusion(bf16[1,2048,1024]{2,1,0:T(8,128)(2,1)} %all-gather.8.cloned.1.call-done, f32[512,2048]{1,0:T(8,128)} %all-reduce.2.cloned.1.call-done, f32[512,2048]{1,0:T(8,128)} %fusion.3), kind=kOutput, calls=%fused_computation | convolution fusion | flops 12885950464 | bytes 14680064 | tf_op jit(solution)/shard_map/dot_general | solution.py:28
  286.7 2.0 add_bitcast_fusion
  (2 shorter events, 0.0 us)
Async XLA Ops:
  6.5 11.8 %copy-start = (bf16[1,128,4096]{2,1,0:T(8,128)(2,1)S(1)}, bf16[1,128,4096]{2,1,0:T(8,128)(2,1)}, u32[]{:S(2)}) copy-start(bf16[1,128,4096]{2,1,0:T(8,128)(2,1)} %param.11) | copy-start | bytes 3145732
  6.5 76.1 %all-gather.6.cloned.1.call-start = ((), (), s32[]{:S(2)}) async-start(), calls=%async_computation.2 | async-start | bytes 2621440 | tf_op jit(solution)/shard_map/all_gather | solution.py:20
  16.9 223.5 %all-reduce.2.cloned.1.call-start = ((), (), s32[]{:S(2)}) async-start(), calls=%async_computation.1 | async-start | bytes 8388608 | tf_op jit(solution)/shard_map/psum | solution.py:17
  16.9 7.2 %copy-start.2 = (f32[1,128]{1,0:T(1,128)S(1)}, f32[1,128]{1,0:T(1,128)}, u32[]{:S(2)}) copy-start(f32[1,128]{1,0:T(1,128)} %param.8) | copy-start | bytes 1540
  16.9 7.2 %copy-start.1 = (bf16[1,512,128]{2,1,0:T(8,128)(2,1)S(1)}, bf16[1,512,128]{2,1,0:T(8,128)(2,1)}, u32[]{:S(2)}) copy-start(bf16[1,512,128]{2,1,0:T(8,128)(2,1)} %param.7) | copy-start | bytes 393220
  17.6 258.6 %all-gather.8.cloned.1.call-start = ((), (), s32[]{:S(2)}) async-start(), calls=%async_computation.3 | async-start | bytes 5242880 | tf_op jit(solution)/shard_map/all_gather | solution.py:27
  19.7 62.4 %all-to-all-start = ((bf16[4,128,1024]{1,2,0:T(8,128)(2,1)}), bf16[4,128,1024]{1,2,0:T(8,128)(2,1)S(1)}, u32[]{:S(2)}, u32[]{:S(2)}) async-start(bf16[4,128,1024]{1,2,0:T(8,128)(2,1)} %bitcast.4), calls=%async_computation | async-start | bytes 2097152 | tf_op jit(solution)/shard_map/all_to_all | solution.py:25
Sparse Core Ops, SparseCore 0:
  17.0 65.2 all-gather.5
  84.7 155.6 all-reduce.1
  241.9 34.2 all-gather.7
